TPU v7x, 512 devices: a whole 4x8x8 slice. The times are simulated.
512 devices in a mesh: req: 64 (over y, z), tp: 8 (over x, core).
Axes of the slice: x: 4, y: 8, z: 8, core: 2. Of those that a mesh axis runs over, the one named last changes fastest.
Arguments:
- hidden_in: bfloat16 [64, 512, 1024], P(None, 'req', 'tp'), may hold values from -64 to 64
- cache_keys: bfloat16 [64, 512, 1024], P('req', None, 'tp'), may hold values from -250 to 250
- cache_values: bfloat16 [64, 512, 1024], P('req', None, 'tp'), may hold values from -6 to 6
- cache_lengths: int32 [64], replicated, may hold values from 32 to 512, as said below
- owner_order: int32 [64], replicated, may hold values from 0 to 63, as said below
- request_slot: int32 [64], replicated, may hold values from 0 to 63, as said below
- proj_weight: bfloat16 [3, 1024, 1024], P(None, None, 'tp'), may hold values from -0.0625 to 0.0625
- proj_bias: bfloat16 [3, 1024], P(None, 'tp'), may hold values from -1.5 to 1.5
- output_weight: bfloat16 [1024, 1024], P('tp'), may hold values from -0.75 to 0.75
- output_bias: bfloat16 [1024], replicated, may hold values from -2.5 to 2.5
- norm_gains: bfloat16 [2, 1024], replicated, may hold values from 0.5 to 1.5
- norm_biases: bfloat16 [2, 1024], replicated, may hold values from -2.5 to 2.5
- widen_weight: bfloat16 [1024, 4096], P(None, 'tp'), may hold values from -0.1875 to 0.1875
- widen_bias: bfloat16 [4096], P('tp'), may hold values from -2.5 to 2.5
- narrow_weight: bfloat16 [4096, 1024], P('tp'), may hold values from -0.09375 to 0.09375
- narrow_bias: bfloat16 [1024], replicated, may hold values from -2.5 to 2.5
Outputs:
- hidden_out: bfloat16 [64, 512, 1024], P(None, 'req', 'tp')
- new_cache: bfloat16 [2, 64, 512, 1024], P(None, 'req', None, 'tp')
Inputs may be any that keep to these rules, and one draw needn't show every extreme that they name: owner_order is a permutation of the requests; owner slot s lies on index s // 1 of req. request_slot[owner_order[s]] = s for every slot s. `cache_lengths`: given in request order; the longest is exactly 512.
All inputs are finite; a program needn't handle non-finite values.
Results may differ from a plain program's by a relative error of at most 0.014.
Values may be sent and summed in bfloat16 or wider, within the bound.
No kernel may reach another device: no remote copies, remote signals or barrier semaphores. Data moves between devices by JAX's collectives and lax.ppermute only.
A program may use at most 64 MiB of HBM per device.

v0:
```python
import jax
import jax.numpy as jnp
from jax import lax
from jax.sharding import PartitionSpec as P

HD = 64


def layer_norm(values, scale_row, shift_row):
    average = jnp.mean(values, axis=-1, keepdims=True)
    centred = values - average
    spread = jnp.mean(centred * centred, axis=-1, keepdims=True)
    return centred * lax.rsqrt(spread + 1e-05) * scale_row.astype(jnp.float32) + shift_row.astype(
        jnp.float32
    )


def split_heads(rows_block):
    return rows_block.reshape(rows_block.shape[0], -1, HD)


def block_scores(query_heads, keys_block, allowed):
    scores = jnp.einsum(
        "thd,shd->hts", query_heads, split_heads(keys_block), preferred_element_type=jnp.float32
    )
    return jnp.where(allowed[None], scores, -jnp.inf)


def to_rows(factor):
    return jnp.transpose(factor, (1, 0, 2))


def slot_attention(fields):
    query_rows, key_rows, value_rows, slot_keys, slot_values, length = fields
    fresh_len = query_rows.shape[0]
    block_len = min(512, slot_keys.shape[0])
    block_count = slot_keys.shape[0] // block_len
    query_heads = split_heads(query_rows)
    self_mask = jnp.arange(fresh_len)[:, None] >= jnp.arange(fresh_len)[None, :]
    self_scores = block_scores(query_heads, key_rows, self_mask)
    row_top = jnp.max(self_scores, axis=2, keepdims=True)
    raised = jnp.exp(self_scores - row_top)
    row_total = jnp.sum(raised, axis=2, keepdims=True)
    context = jnp.einsum(
        "hts,shd->thd",
        raised.astype(jnp.bfloat16),
        split_heads(value_rows),
        preferred_element_type=jnp.float32,
    )
    positions = jnp.arange(block_len)

    def one_block(number, carry):
        old_top, old_total, running = carry
        begin_at = number * block_len
        allowed = jnp.broadcast_to((begin_at + positions < length)[None, :], (fresh_len, block_len))
        scores = block_scores(query_heads, slot_keys, allowed)
        new_top = jnp.maximum(old_top, jnp.max(scores, axis=2, keepdims=True))
        factor = jnp.exp(old_top - new_top)
        block_raised = jnp.exp(scores - new_top)
        new_total = old_total * factor + jnp.sum(block_raised, axis=2, keepdims=True)
        added = jnp.einsum(
            "hts,shd->thd",
            block_raised.astype(jnp.bfloat16),
            split_heads(slot_values),
            preferred_element_type=jnp.float32,
        )
        return (new_top, new_total, running * to_rows(factor) + added)

    row_top, row_total, context = lax.fori_loop(
        0, block_count, one_block, (row_top, row_total, context)
    )
    context = context / to_rows(row_total)
    return context.reshape(fresh_len, -1).astype(jnp.bfloat16)


def widen_rows(normed, widen_weight, widen_bias):
    widened = jnp.dot(normed, widen_weight, preferred_element_type=jnp.float32) + widen_bias.astype(
        jnp.float32
    )
    return jax.nn.gelu(widened, approximate=False).astype(jnp.bfloat16)


def on_device(
    hidden_in,
    cache_keys,
    cache_values,
    cache_lengths,
    owner_order,
    request_slot,
    proj_weight,
    proj_bias,
    output_weight,
    output_bias,
    norm_gains,
    norm_biases,
    widen_weight,
    widen_bias,
    narrow_weight,
    narrow_bias,
):
    slot_count = cache_keys.shape[0]
    fresh_len = hidden_in.shape[1] * lax.axis_size("req")
    owned_slots = lax.dynamic_slice_in_dim(
        owner_order, lax.axis_index("req") * slot_count, slot_count
    )
    lengths = jnp.take(cache_lengths, owned_slots)
    gathered = lax.all_gather(hidden_in, "tp", axis=2, tiled=True)
    token_rows = lax.all_to_all(
        jnp.take(gathered, owner_order, axis=0), "req", split_axis=0, concat_axis=1, tiled=True
    )
    flat_rows = token_rows.reshape(slot_count * fresh_len, -1)
    projected = (
        jnp.einsum("td,cdf->ctf", flat_rows, proj_weight, preferred_element_type=jnp.float32)
        + proj_bias.astype(jnp.float32)[:, None, :]
    )
    query_rows = (
        (projected[0] * HD ** (-0.5)).astype(jnp.bfloat16).reshape(slot_count, fresh_len, -1)
    )
    key_rows = projected[1].astype(jnp.bfloat16).reshape(slot_count, fresh_len, -1)
    value_rows = projected[2].astype(jnp.bfloat16).reshape(slot_count, fresh_len, -1)
    new_cache = jnp.stack([key_rows, value_rows], axis=0)
    context = lax.map(
        slot_attention, (query_rows, key_rows, value_rows, cache_keys, cache_values, lengths)
    )
    context = context.reshape(slot_count * fresh_len, -1)
    tp_count = lax.axis_size("tp")
    attended = lax.psum(
        jnp.dot(context, output_weight, preferred_element_type=jnp.float32).astype(jnp.bfloat16),
        "tp",
    ).astype(jnp.float32)
    normed = layer_norm(
        flat_rows.astype(jnp.float32) + attended + output_bias.astype(jnp.float32),
        norm_gains[0],
        norm_biases[0],
    ).astype(jnp.bfloat16)
    activated = widen_rows(normed, widen_weight, widen_bias)
    fed_total = lax.psum(
        jnp.dot(activated, narrow_weight, preferred_element_type=jnp.float32).astype(jnp.bfloat16),
        "tp",
    ).astype(jnp.float32)
    updated = layer_norm(
        normed.astype(jnp.float32) + fed_total + narrow_bias.astype(jnp.float32),
        norm_gains[1],
        norm_biases[1],
    ).astype(jnp.bfloat16)
    column_count = updated.shape[1] // tp_count
    updated = lax.dynamic_slice_in_dim(
        updated, lax.axis_index("tp") * column_count, column_count, 1
    )
    returned = lax.all_to_all(
        updated.reshape(slot_count, fresh_len, -1), "req", split_axis=1, concat_axis=0, tiled=True
    )
    hidden_out = jnp.take(returned, request_slot, axis=0)
    return (hidden_out, new_cache)


def solution(mesh):
    in_specs = (
        P(None, "req", "tp"),
        P("req", None, "tp"),
        P("req", None, "tp"),
        P(),
        P(),
        P(),
        P(None, None, "tp"),
        P(None, "tp"),
        P("tp", None),
        P(),
        P(),
        P(),
        P(None, "tp"),
        P("tp"),
        P("tp", None),
        P(),
    )
    out_specs = (P(None, "req", "tp"), P(None, "req", None, "tp"))
    return jax.shard_map(
        on_device, mesh=mesh, in_specs=in_specs, out_specs=out_specs, check_vma=False
    )
```

profile of v0, /device:TPU:8, one launch (start us, length us, event | category | flops | bytes accessed | tf_op | source)
XLA Modules:
  0.0 283.8 jit_solution(11562906684038777593)
XLA Ops:
  7.2 0.7 all-gather.2.cloned.1.call-update
  7.9 0.7 compare_select_fusion
  8.6 0.7 compare_and_fusion
  9.2 34.1 %all-gather.2.cloned.1.call-done = bf16[64,8,1024]{2,1,0:T(8,128)(2,1)} async-done(((bf16[64,8,128]{2,1,0:T(8,128)(2,1)}), bf16[64,8,1024]{2,1,0:T(8,128)(2,1)}) %all-gather.2.cloned.1.call-update) | async-done | bytes 1048592 | tf_op jit(solution)/shard_map/all_gather | solution.py:107
  43.3 1.8 gather_fusion
  45.2 1.1 broadcast_select_fusion
  46.3 13.5 %all-to-all-start = ((bf16[64,8,1024]{2,1,0:T(8,128)(2,1)}), bf16[64,8,1024]{2,1,0:T(8,128)(2,1)S(1)}, u32[]{:S(2)}, u32[]{:S(2)}) async-start(bf16[64,8,1024]{2,1,0:T(8,128)(2,1)} %broadcast_select_fusion), calls=%async_computation | async-start | bytes 2097152 | tf_op jit(solution)/shard_map/all_to_all | solution.py:108
  62.6 1.4 copy.36
  64.0 0.8 copy.38
  66.2 23.3 %all-to-all-done = bf16[64,8,1024]{2,1,0:T(8,128)(2,1)S(1)} async-done(((bf16[64,8,1024]{2,1,0:T(8,128)(2,1)}), bf16[64,8,1024]{2,1,0:T(8,128)(2,1)S(1)}, u32[]{:S(2)}, u32[]{:S(2)}) %all-to-all-start) | async-done | bytes 1048608 | tf_op jit(solution)/shard_map/all_to_all | solution.py:108
  92.1 0.9 fusion.2
  93.0 0.7 fusion.10
  93.9 1.5 convolution_convert_fusion
  95.8 68.0 %all-reduce.3.cloned.1.call-done = bf16[512,1024]{1,0:T(8,128)(2,1)} async-done(((bf16[512,1024]{1,0:T(8,128)(2,1)}), bf16[512,1024]{1,0:T(8,128)(2,1)}) %all-reduce.3.cloned.1.call-update) | async-done | bytes 1048592 | tf_op jit(solution)/shard_map/psum | solution.py:127
  163.8 1.7 fusion.6
  166.7 5.6 %convolution_convert_fusion.1 = bf16[512,1024]{1,0:T(8,128)(2,1)} fusion(bf16[512,1024]{1,0:T(8,128)(2,1)S(1)} %copy-done, bf16[512,1024]{1,0:T(8,128)(2,1)S(1)} %add_convert_fusion, bf16[1024,512]{1,0:T(8,128)(2,1)} %param.28, f32[512]{0:T(512)S(1)} %convert_element_type.122), kind=kOutput, calls=%fused_computation.20 | convolution fusion | flops 1091567616 | bytes 4196352 | tf_op jit(solution)/shard_map/dot_general | solution.py:138
  172.6 72.7 %all-reduce.5.cloned.1.call-done = bf16[512,1024]{1,0:T(8,128)(2,1)} async-done(((bf16[512,1024]{1,0:T(8,128)(2,1)}), bf16[512,1024]{1,0:T(8,128)(2,1)}) %all-reduce.5.cloned.1.call-update) | async-done | bytes 1048592 | tf_op jit(solution)/shard_map/psum | solution.py:137
  245.3 1.7 fusion.1
  248.5 1.4 reduce
  249.9 0.7 reshape.238
  250.6 13.4 %all-to-all-start.1 = ((bf16[64,2,512]{2,1,0:T(2,128)(2,1)}), bf16[64,2,512]{2,1,0:T(2,128)(2,1)S(1)}, u32[]{:S(2)}, u32[]{:S(2)}) async-start(bf16[64,2,512]{2,1,0:T(2,128)(2,1)} %reshape.238), calls=%async_computation.1 | async-start | bytes 262144 | tf_op jit(solution)/shard_map/all_to_all | solution.py:150
  264.0 0.8 copy.42
  264.9 10.8 %all-to-all-done.1 = bf16[64,2,512]{2,1,0:T(2,128)(2,1)S(1)} async-done(((bf16[64,2,512]{2,1,0:T(2,128)(2,1)}), bf16[64,2,512]{2,1,0:T(2,128)(2,1)S(1)}, u32[]{:S(2)}, u32[]{:S(2)}) %all-to-all-start.1) | async-done | bytes 131104 | tf_op jit(solution)/shard_map/all_to_all | solution.py:150
  276.5 0.8 broadcast_select_fusion.1
  (77 shorter events, 8.2 us)
Async XLA Ops:
  7.2 159.5 %copy-start = (bf16[512,1024]{1,0:T(8,128)(2,1)S(1)}, bf16[512,1024]{1,0:T(8,128)(2,1)}, u32[]{:S(2)}) copy-start(bf16[512,1024]{1,0:T(8,128)(2,1)} %param.30) | copy-start | bytes 3145732
  7.2 36.1 %all-gather.2.cloned.1.call-start = ((), (), s32[]{:S(2)}) async-start(), calls=%async_computation.2 | async-start | bytes 1179648 | tf_op jit(solution)/shard_map/all_gather | solution.py:107
  45.1 14.7 %copy-start.5 = (bf16[1,512,128]{2,1,0:T(8,128)(2,1)S(1)}, bf16[1,512,128]{2,1,0:T(8,128)(2,1)}, u32[]{:S(2)}) copy-start(bf16[1,512,128]{2,1,0:T(8,128)(2,1)} %param.18) | copy-start | bytes 393220
  45.2 14.9 %copy-start.13 = (s32[64]{0:T(128)S(1)}, s32[64]{0:T(128)}, u32[]{:S(2)}) copy-start(s32[64]{0:T(128)} %param.20) | copy-start | bytes 772
  46.3 17.7 %copy-start.11 = (bf16[3,128]{1,0:T(4,128)(2,1)S(1)}, bf16[3,128]{1,0:T(4,128)(2,1)}, u32[]{:S(2)}) copy-start(bf16[3,128]{1,0:T(4,128)(2,1)} %param.23) | copy-start | bytes 2308
  46.3 17.7 %copy-start.6 = (bf16[1,512,128]{2,1,0:T(8,128)(2,1)S(1)}, bf16[1,512,128]{2,1,0:T(8,128)(2,1)}, u32[]{:S(2)}) copy-start(bf16[1,512,128]{2,1,0:T(8,128)(2,1)} %param.17) | copy-start | bytes 393220
  46.3 18.5 %copy-start.14 = (s32[64]{0:T(128)S(1)}, s32[64]{0:T(128)}, u32[]{:S(2)}) copy-start(s32[64]{0:T(128)} %param.19) | copy-start | bytes 772
  46.3 43.2 %all-to-all-start = ((bf16[64,8,1024]{2,1,0:T(8,128)(2,1)}), bf16[64,8,1024]{2,1,0:T(8,128)(2,1)S(1)}, u32[]{:S(2)}, u32[]{:S(2)}) async-start(bf16[64,8,1024]{2,1,0:T(8,128)(2,1)} %broadcast_select_fusion), calls=%async_computation | async-start | bytes 2097152 | tf_op jit(solution)/shard_map/all_to_all | solution.py:108
  59.8 103.9 %all-reduce.3.cloned.1.call-start = ((), (), s32[]{:S(2)}) async-start(), calls=%async_computation.3 | async-start | bytes 2097152 | tf_op jit(solution)/shard_map/psum | solution.py:127
  89.5 0.9 copy-start.3
  93.0 1.0 copy-start.4
  93.7 2.0 copy-start.9
  93.7 2.0 copy-start.12
  93.7 2.0 copy-start.7
  93.7 2.0 copy-start.8
  95.4 149.8 %all-reduce.5.cloned.1.call-start = ((), (), s32[]{:S(2)}) async-start(), calls=%async_computation.4 | async-start | bytes 2097152 | tf_op jit(solution)/shard_map/psum | solution.py:137
  163.8 1.7 copy-start.1
  166.7 5.7 %copy-start.10 = (bf16[1024]{0:T(1024)(128)(2,1)S(1)}, bf16[1024]{0:T(1024)(128)(2,1)}, u32[]{:S(2)}) copy-start(bf16[1024]{0:T(1024)(128)(2,1)} %param.31) | copy-start | bytes 6148
  166.7 5.9 %copy-start.15 = (s32[64]{0:T(128)S(1)}, s32[64]{0:T(128)}, u32[]{:S(2)}) copy-start(s32[64]{0:T(128)} %param.21) | copy-start | bytes 772
  245.3 1.7 copy-start.2
  250.6 25.1 %all-to-all-start.1 = ((bf16[64,2,512]{2,1,0:T(2,128)(2,1)}), bf16[64,2,512]{2,1,0:T(2,128)(2,1)S(1)}, u32[]{:S(2)}, u32[]{:S(2)}) async-start(bf16[64,2,512]{2,1,0:T(2,128)(2,1)} %reshape.238), calls=%async_computation.1 | async-start | bytes 262144 | tf_op jit(solution)/shard_map/all_to_all | solution.py:150
Sparse Core Ops, SparseCore 0:
  10.1 33.1 all-gather.1
  95.6 68.1 all-reduce.2
  172.5 72.6 all-reduce.4
where the time goes:
time: 284 us
  waiting for transfers between devices  210 us (74%)
  starting transfers between devices  27.2 us (10%)
  between operations  16.8 us (6%)
  other arithmetic  11.2 us (4%)
  matrix products  10 us (4%)
  local copies, waits for them, and re-layouts  8.95 us (3%)
    psum x1, waiting for transfers between devices, on_device(): lax.psum(jnp.dot(activated, narrow_weight, preferred_element_type=jnp.flo...  72.7 us
    psum x1, waiting for transfers between devices, on_device(): lax.psum(jnp.dot(context, output_weight, preferred_element_type=jnp.float...  68 us
    all_gather x1, waiting for transfers between devices, on_device(): gathered = lax.all_gather(hidden_in, 'tp', axis=2, tiled=True)  34.1 us
    all_to_all x1, waiting for transfers between devices, on_device(): lax.all_to_all(jnp.take(gathered, owner_order, axis=0), 'req', split_axis...  23.3 us
    all_to_all x1, starting transfers between devices, on_device(): lax.all_to_all(jnp.take(gathered, owner_order, axis=0), 'req', split_axis...  13.5 us
    all_to_all x1, starting transfers between devices, on_device(): lax.all_to_all(updated.reshape(slot_count, fresh_len, -1), 'req', split_a...  13.4 us
    all_to_all x1, waiting for transfers between devices, on_device(): lax.all_to_all(updated.reshape(slot_count, fresh_len, -1), 'req', split_a...  10.8 us
  transfers between devices with their start and end apart: 5, of which 5 were waited for; matrix products, arithmetic and copies ran while one was open for 2% of the time, Pallas kernels for 0%

commit v1 on v0

--- a/solution.py
+++ b/solution.py
@@ -134,9 +134,14 @@
         norm_biases[0],
     ).astype(jnp.bfloat16)
     activated = widen_rows(normed, widen_weight, widen_bias)
-    fed_total = lax.psum(
-        jnp.dot(activated, narrow_weight, preferred_element_type=jnp.float32).astype(jnp.bfloat16),
-        "tp",
+    fed_total = jnp.sum(
+        jax.lax.all_gather(
+            jnp.dot(activated, narrow_weight, preferred_element_type=jnp.float32).astype(
+                jnp.bfloat16
+            ),
+            "tp",
+        ),
+        axis=0,
     ).astype(jnp.float32)
     updated = layer_norm(
         normed.astype(jnp.float32) + fed_total + narrow_bias.astype(jnp.float32),

time: 284 us -> 271 us (0.954)
  the two profiles are of different devices: /device:TPU:8 before, /device:TPU:1 now
where the time goes in v1:
time: 271 us
  waiting for transfers between devices  193 us (71%)
  starting transfers between devices  26.5 us (10%)
  between operations  16.7 us (6%)
  other arithmetic  15.6 us (6%)
  matrix products  10.1 us (4%)
  local copies, waits for them, and re-layouts  8.86 us (3%)
    psum x1, waiting for transfers between devices, on_device(): lax.psum(jnp.dot(context, output_weight, preferred_element_type=jnp.float...  69.1 us
    all_gather x1, waiting for transfers between devices, on_device(): jax.lax.all_gather(jnp.dot(activated, narrow_weight, preferred_element_ty...  56.3 us
    all_gather x1, waiting for transfers between devices, on_device(): gathered = lax.all_gather(hidden_in, 'tp', axis=2, tiled=True)  35.4 us
    all_to_all x1, waiting for transfers between devices, on_device(): lax.all_to_all(jnp.take(gathered, owner_order, axis=0), 'req', split_axis...  21 us
    all_to_all x1, starting transfers between devices, on_device(): lax.all_to_all(jnp.take(gathered, owner_order, axis=0), 'req', split_axis...  13.1 us
    all_to_all x1, starting transfers between devices, on_device(): lax.all_to_all(updated.reshape(slot_count, fresh_len, -1), 'req', split_a...  13 us
    all_to_all x1, waiting for transfers between devices, on_device(): lax.all_to_all(updated.reshape(slot_count, fresh_len, -1), 'req', split_a...  10.6 us
    dot_general x1, matrix products, on_device(): jnp.dot(activated, narrow_weight, preferred_element_type=jnp.float32)  5.68 us
  transfers between devices with their start and end apart: 5, of which 5 were waited for; matrix products, arithmetic and copies ran while one was open for 2% of the time, Pallas kernels for 0%

profile of v1, /device:TPU:1, one launch (start us, length us, event | category | flops | bytes accessed | tf_op | source)
XLA Modules:
  0.0 270.7 jit_solution(16115705989915387815)
XLA Ops:
  7.2 0.7 all-gather.4.cloned.1.call-update
  7.9 0.7 compare_select_fusion
  8.6 0.7 compare_and_fusion
  9.2 35.4 %all-gather.4.cloned.1.call-done = bf16[64,8,1024]{2,1,0:T(8,128)(2,1)} async-done(((bf16[64,8,128]{2,1,0:T(8,128)(2,1)}), bf16[64,8,1024]{2,1,0:T(8,128)(2,1)}) %all-gather.4.cloned.1.call-update) | async-done | bytes 1048592 | tf_op jit(solution)/shard_map/all_gather | solution.py:107
  44.6 1.8 gather_fusion
  46.5 1.1 broadcast_select_fusion
  47.6 13.1 %all-to-all-start = ((bf16[64,8,1024]{2,1,0:T(8,128)(2,1)}), bf16[64,8,1024]{2,1,0:T(8,128)(2,1)S(1)}, u32[]{:S(2)}, u32[]{:S(2)}) async-start(bf16[64,8,1024]{2,1,0:T(8,128)(2,1)} %broadcast_select_fusion), calls=%async_computation | async-start | bytes 2097152 | tf_op jit(solution)/shard_map/all_to_all | solution.py:108
  63.4 1.4 copy.36
  64.8 0.8 copy.38
  67.0 21.0 %all-to-all-done = bf16[64,8,1024]{2,1,0:T(8,128)(2,1)S(1)} async-done(((bf16[64,8,1024]{2,1,0:T(8,128)(2,1)}), bf16[64,8,1024]{2,1,0:T(8,128)(2,1)S(1)}, u32[]{:S(2)}, u32[]{:S(2)}) %all-to-all-start) | async-done | bytes 1048608 | tf_op jit(solution)/shard_map/all_to_all | solution.py:108
  89.9 0.9 fusion.2
  91.4 0.7 fusion.10
  92.3 1.5 convolution_convert_fusion
  94.2 69.1 %all-reduce.2.cloned.1.call-done = bf16[512,1024]{1,0:T(8,128)(2,1)} async-done(((bf16[512,1024]{1,0:T(8,128)(2,1)}), bf16[512,1024]{1,0:T(8,128)(2,1)}) %all-reduce.2.cloned.1.call-update) | async-done | bytes 1048592 | tf_op jit(solution)/shard_map/psum | solution.py:127
  163.3 1.7 fusion.6
  166.2 5.7 %convolution_convert_fusion.1 = bf16[512,1024]{1,0:T(8,128)(2,1)} fusion(bf16[512,1024]{1,0:T(8,128)(2,1)S(1)} %copy-done, bf16[512,1024]{1,0:T(8,128)(2,1)S(1)} %add_convert_fusion, bf16[1024,512]{1,0:T(8,128)(2,1)} %param.28, f32[512]{0:T(512)S(1)} %convert_element_type.124), kind=kOutput, calls=%fused_computation.20 | convolution fusion | flops 1091567616 | bytes 4196352 | tf_op jit(solution)/shard_map/dot_general | solution.py:139
  172.1 56.3 %all-gather.6.cloned.1.call-done = bf16[4096,1024]{1,0:T(8,128)(2,1)} async-done(((bf16[512,1024]{1,0:T(8,128)(2,1)}), bf16[4096,1024]{1,0:T(8,128)(2,1)}) %all-gather.6.cloned.1.call-update) | async-done | bytes 8388624 | tf_op jit(solution)/shard_map/all_gather | solution.py:138
  228.4 5.7 %reduce_sum.79 = bf16[512,1024]{1,0:T(8,128)(2,1)S(1)} reduce(bf16[8,512,1024]{2,1,0:T(8,128)(2,1)} %bitcast.88, bf16[]{:T(256)} %constant.161.clone.1), dimensions={0}, to_apply=%region_7.8 | reduce | flops 3670016 | bytes 9437186 | tf_op jit(solution)/shard_map/reduce_sum | solution.py:137
  235.9 1.4 reduce.1
  237.4 0.7 reshape.239
  238.1 13.0 %all-to-all-start.1 = ((bf16[64,2,512]{2,1,0:T(2,128)(2,1)}), bf16[64,2,512]{2,1,0:T(2,128)(2,1)S(1)}, u32[]{:S(2)}, u32[]{:S(2)}) async-start(bf16[64,2,512]{2,1,0:T(2,128)(2,1)} %reshape.239), calls=%async_computation.1 | async-start | bytes 262144 | tf_op jit(solution)/shard_map/all_to_all | solution.py:155
  251.1 0.8 copy.42
  252.0 10.6 %all-to-all-done.1 = bf16[64,2,512]{2,1,0:T(2,128)(2,1)S(1)} async-done(((bf16[64,2,512]{2,1,0:T(2,128)(2,1)}), bf16[64,2,512]{2,1,0:T(2,128)(2,1)S(1)}, u32[]{:S(2)}, u32[]{:S(2)}) %all-to-all-start.1) | async-done | bytes 131104 | tf_op jit(solution)/shard_map/all_to_all | solution.py:155
  263.3 0.8 broadcast_select_fusion.1
  (76 shorter events, 8.5 us)
Async XLA Ops:
  7.2 159.0 %copy-start = (bf16[512,1024]{1,0:T(8,128)(2,1)S(1)}, bf16[512,1024]{1,0:T(8,128)(2,1)}, u32[]{:S(2)}) copy-start(bf16[512,1024]{1,0:T(8,128)(2,1)} %param.30) | copy-start | bytes 3145732
  7.2 37.4 %all-gather.4.cloned.1.call-start = ((), (), s32[]{:S(2)}) async-start(), calls=%async_computation.2 | async-start | bytes 1179648 | tf_op jit(solution)/shard_map/all_gather | solution.py:107
  46.4 14.4 %copy-start.12 = (s32[64]{0:T(128)S(1)}, s32[64]{0:T(128)}, u32[]{:S(2)}) copy-start(s32[64]{0:T(128)} %param.20) | copy-start | bytes 772
  47.6 17.2 %copy-start.10 = (bf16[3,128]{1,0:T(4,128)(2,1)S(1)}, bf16[3,128]{1,0:T(4,128)(2,1)}, u32[]{:S(2)}) copy-start(bf16[3,128]{1,0:T(4,128)(2,1)} %param.23) | copy-start | bytes 2308
  47.6 17.2 %copy-start.4 = (bf16[1,512,128]{2,1,0:T(8,128)(2,1)S(1)}, bf16[1,512,128]{2,1,0:T(8,128)(2,1)}, u32[]{:S(2)}) copy-start(bf16[1,512,128]{2,1,0:T(8,128)(2,1)} %param.17) | copy-start | bytes 393220
  47.6 18.0 %copy-start.5 = (bf16[1,512,128]{2,1,0:T(8,128)(2,1)S(1)}, bf16[1,512,128]{2,1,0:T(8,128)(2,1)}, u32[]{:S(2)}) copy-start(bf16[1,512,128]{2,1,0:T(8,128)(2,1)} %param.18) | copy-start | bytes 393220
  47.6 18.1 %copy-start.13 = (s32[64]{0:T(128)S(1)}, s32[64]{0:T(128)}, u32[]{:S(2)}) copy-start(s32[64]{0:T(128)} %param.19) | copy-start | bytes 772
  47.6 40.3 %all-to-all-start = ((bf16[64,8,1024]{2,1,0:T(8,128)(2,1)}), bf16[64,8,1024]{2,1,0:T(8,128)(2,1)S(1)}, u32[]{:S(2)}, u32[]{:S(2)}) async-start(bf16[64,8,1024]{2,1,0:T(8,128)(2,1)} %broadcast_select_fusion), calls=%async_computation | async-start | bytes 2097152 | tf_op jit(solution)/shard_map/all_to_all | solution.py:108
  60.8 102.5 %all-reduce.2.cloned.1.call-start = ((), (), s32[]{:S(2)}) async-start(), calls=%async_computation.3 | async-start | bytes 2097152 | tf_op jit(solution)/shard_map/psum | solution.py:127
  87.9 0.9 copy-start.2
  91.4 1.0 copy-start.3
  92.1 2.0 copy-start.8
  92.1 2.0 copy-start.11
  92.1 2.0 copy-start.6
  92.1 2.0 copy-start.7
  93.8 134.6 %all-gather.6.cloned.1.call-start = ((), (), s32[]{:S(2)}) async-start(), calls=%async_computation.4 | async-start | bytes 9437184 | tf_op jit(solution)/shard_map/all_gather | solution.py:138
  163.3 1.7 copy-start.1
  166.2 5.7 %copy-start.9 = (bf16[1024]{0:T(1024)(128)(2,1)S(1)}, bf16[1024]{0:T(1024)(128)(2,1)}, u32[]{:S(2)}) copy-start(bf16[1024]{0:T(1024)(128)(2,1)} %param.31) | copy-start | bytes 6148
  166.2 5.9 %copy-start.14 = (s32[64]{0:T(128)S(1)}, s32[64]{0:T(128)}, u32[]{:S(2)}) copy-start(s32[64]{0:T(128)} %param.21) | copy-start | bytes 772
  238.1 24.5 %all-to-all-start.1 = ((bf16[64,2,512]{2,1,0:T(2,128)(2,1)}), bf16[64,2,512]{2,1,0:T(2,128)(2,1)S(1)}, u32[]{:S(2)}, u32[]{:S(2)}) async-start(bf16[64,2,512]{2,1,0:T(2,128)(2,1)} %reshape.239), calls=%async_computation.1 | async-start | bytes 262144 | tf_op jit(solution)/shard_map/all_to_all | solution.py:155
Sparse Core Ops, SparseCore 0:
  10.1 34.4 all-gather.3
  94.0 69.2 all-reduce.1
  172.1 56.2 all-gather.5
